TPU v7x, 256 devices: a whole 4x4x8 slice. The times are simulated.
256 devices in a mesh: blk: 4 (over y_hi, core), reader: 8 (over y_lo, x), bulk: 8 (over z).
Axes of the slice: x: 4, y: 4 (y_hi: 2, y_lo: 2; y = y_hi * 2 + y_lo), z: 8, core: 2. Of those that a mesh axis runs over, the one named last changes fastest.
Arguments:
- vectors: float32 [128, 32768], P('bulk', ('blk', 'reader')), may hold values from -6 to 6
- ham_tiles: float32 [32, 4, 24, 128, 128], P(('blk', 'reader'))
- tile_rows: int32 [32, 4, 24], P(('blk', 'reader')), may hold values from 0 to 7, as said below
- tile_cols: int32 [32, 4, 24], P(('blk', 'reader')), may hold values from 0 to 63
- center: float32 [1], replicated, may hold values from -0.5 to 0.5
- halfwidth: float32 [1], replicated, may hold values from 1 to 2
Outputs:
- filtered: float32 [128, 32768], P('bulk', ('blk', 'reader'))
Inputs may be any that keep to these rules, and one draw needn't show every extreme that they name: tile_rows and tile_cols of one panel together name 24 different tiles.
All inputs are finite; a program needn't handle non-finite values.
Results may differ from a plain program's by a relative error of at most 0.0003.
Values sent between devices are 32-bit elements; how exact they have to be, the bound alone decides.
No kernel may reach another device: no remote copies, remote signals or barrier semaphores. Data moves between devices by JAX's collectives and lax.ppermute only.
A program may use at most 64 MiB of HBM per device.

v0:
```python
import jax
import jax.numpy as jnp
from jax import lax
from jax.sharding import PartitionSpec as P

TILE = 128
PASSES = 2


def contribute(sources, tiles, rows, count):
    product = jnp.einsum("vkc,krc->vkr", sources, tiles, precision=lax.Precision.HIGHEST)
    onehot = (rows[:, None] == jnp.arange(count, dtype=jnp.int32)[None, :]).astype(jnp.float32)
    return jnp.einsum("vkr,kt->vtr", product, onehot, precision=lax.Precision.HIGHEST)


def apply_ham(current, tiles_here, rows_here, cols_here):
    local_vecs = current.shape[0]
    row_tiles = current.shape[1] // TILE
    groups = tiles_here.shape[0]
    slots = tiles_here.shape[1]
    group_tiles = lax.axis_size("reader") * row_tiles
    whole = lax.all_gather(current, ("blk", "reader"), axis=1, tiled=True)
    tiled = whole.reshape(local_vecs, whole.shape[1] // TILE, TILE)
    offsets = (jnp.arange(groups, dtype=jnp.int32) * group_tiles)[:, None]
    glob = (offsets + cols_here).reshape(-1)
    sources = jnp.take(tiled, glob, axis=1)
    total = contribute(
        sources, tiles_here.reshape(groups * slots, TILE, TILE), rows_here.reshape(-1), row_tiles
    )
    return total.reshape(local_vecs, row_tiles * TILE)


def shards(vectors, ham_tiles, tile_rows, tile_cols, center, halfwidth):
    tiles_here = ham_tiles[0]
    rows_here = tile_rows[0]
    cols_here = tile_cols[0]
    total_rows = vectors.shape[1] * lax.axis_size("blk") * lax.axis_size("reader")

    def scaled(field):
        return (apply_ham(field, tiles_here, rows_here, cols_here) - center[0] * field) / halfwidth[
            0
        ]

    current = vectors
    for step in range(PASSES):
        first = scaled(current)
        second = 2.0 * scaled(first) - current
        third = 2.0 * scaled(second) - first
        squares = lax.psum(jnp.sum(third * third, axis=1), ("blk", "reader"))
        current = third / jnp.sqrt(squares / total_rows + 1e-06)[:, None]
    return current


def solution(mesh):
    return jax.shard_map(
        shards,
        mesh=mesh,
        in_specs=(
            P("bulk", ("blk", "reader")),
            P(("blk", "reader"), None, None, None, None),
            P(("blk", "reader"), None, None),
            P(("blk", "reader"), None, None),
            P(),
            P(),
        ),
        out_specs=P("bulk", ("blk", "reader")),
        check_vma=False,
    )
```

profile of v0, /device:TPU:32, one launch (start us, length us, event | category | flops | bytes accessed | tf_op | source)
XLA Modules:
  0.0 754.0 jit_solution(11329175917317144318)
XLA Ops:
  8.6 0.8 eq.8
  9.4 0.8 squeeze.6
  10.3 85.0 %all-gather.7.cloned.1.call-done = f32[16,32768]{1,0:T(8,128)} async-done(((f32[16,1024]{1,0:T(8,128)}), f32[16,32768]{1,0:T(8,128)}) %all-gather.7.cloned.1.call-update) | async-done | bytes 2097168 | tf_op jit(solution)/shard_map/all_gather | solution.py:22
  95.3 1.7 copy_bitcast_fusion.5
  97.8 12.0 %convolution_bitcast_fusion.5 = f32[16,96,128]{2,0,1:T(8,128)S(1)} fusion(f32[96,128,128]{2,1,0:T(8,128)} %bitcast.143, f32[96,16,128]{2,1,0:T(8,128)S(1)} %gather_fusion, pred[96]{0:T(512)(128)(4,1)S(1)} %get-tuple-element.10), kind=kOutput, calls=%fused_computation.17 | convolution fusion | flops 302186496 | bytes 7864416 | tf_op jit(solution)/shard_map/vkc,krc->vkr/dot_general | solution.py:11
  111.1 85.4 %all-gather.9.cloned.1.call-done = f32[16,32768]{1,0:T(8,128)} async-done(((f32[16,1024]{1,0:T(8,128)}), f32[16,32768]{1,0:T(8,128)}) %all-gather.9.cloned.1.call-update) | async-done | bytes 2097168 | tf_op jit(solution)/shard_map/all_gather | solution.py:22
  196.5 1.7 copy_bitcast_fusion.4
  199.0 12.0 %convolution_bitcast_fusion.4 = f32[16,96,128]{2,0,1:T(8,128)S(1)} fusion(f32[96,128,128]{2,1,0:T(8,128)} %bitcast.144, f32[96,16,128]{2,1,0:T(8,128)S(1)} %gather_fusion.1, pred[96]{0:T(512)(128)(4,1)S(1)} %get-tuple-element.10), kind=kOutput, calls=%fused_computation.16 | convolution fusion | flops 302186496 | bytes 7864416 | tf_op jit(solution)/shard_map/vkc,krc->vkr/dot_general | solution.py:11
  212.4 85.3 %all-gather.11.cloned.1.call-done = f32[16,32768]{1,0:T(8,128)} async-done(((f32[16,1024]{1,0:T(8,128)}), f32[16,32768]{1,0:T(8,128)}) %all-gather.11.cloned.1.call-update) | async-done | bytes 2097168 | tf_op jit(solution)/shard_map/all_gather | solution.py:22
  297.7 1.7 copy_bitcast_fusion.3
  300.1 12.0 %convolution_bitcast_fusion.3 = f32[16,96,128]{2,0,1:T(8,128)S(1)} fusion(f32[96,128,128]{2,1,0:T(8,128)} %bitcast.145, f32[96,16,128]{2,1,0:T(8,128)S(1)} %gather_fusion.2, pred[96]{0:T(512)(128)(4,1)S(1)} %get-tuple-element.10), kind=kOutput, calls=%fused_computation.15 | convolution fusion | flops 302186496 | bytes 7864416 | tf_op jit(solution)/shard_map/vkc,krc->vkr/dot_general | solution.py:11
  312.8 67.6 %psum.14 = f32[16]{0:T(128)S(1)} all-reduce(f32[16]{0:T(128)S(1)} %get-tuple-element.8), channel_id=1, replica_groups=mesh['blk'=4,'reader'=8,'bulk'=8] {'blk','reader'}, use_global_device_ids=true, to_apply=%region_1.3 | all-reduce | flops 16 | bytes 128 | tf_op jit(solution)/shard_map/psum | solution.py:49
  381.2 80.1 %all-gather.13.cloned.1.call-done = f32[16,32768]{1,0:T(8,128)} async-done(((f32[16,1024]{1,0:T(8,128)}), f32[16,32768]{1,0:T(8,128)}) %all-gather.13.cloned.1.call-update) | async-done | bytes 2097168 | tf_op jit(solution)/shard_map/all_gather | solution.py:22
  461.2 1.7 copy_bitcast_fusion.2
  463.7 11.9 %convolution_bitcast_fusion.2 = f32[16,96,128]{2,0,1:T(8,128)S(1)} fusion(f32[96,128,128]{2,1,0:T(8,128)} %bitcast.146, f32[96,16,128]{2,1,0:T(8,128)S(1)} %gather_fusion.3, pred[96]{0:T(512)(128)(4,1)S(1)} %get-tuple-element.10), kind=kOutput, calls=%fused_computation.14 | convolution fusion | flops 302186496 | bytes 7864416 | tf_op jit(solution)/shard_map/vkc,krc->vkr/dot_general | solution.py:11
  476.2 0.7 fusion.42
  477.2 85.2 %all-gather.15.cloned.1.call-done = f32[16,32768]{1,0:T(8,128)} async-done(((f32[16,1024]{1,0:T(8,128)}), f32[16,32768]{1,0:T(8,128)}) %all-gather.15.cloned.1.call-update) | async-done | bytes 2097168 | tf_op jit(solution)/shard_map/all_gather | solution.py:22
  562.4 1.7 copy_bitcast_fusion.1
  564.9 12.0 %convolution_bitcast_fusion.1 = f32[16,96,128]{2,0,1:T(8,128)S(1)} fusion(f32[96,128,128]{2,1,0:T(8,128)} %bitcast.147, f32[96,16,128]{2,1,0:T(8,128)S(1)} %gather_fusion.4, pred[96]{0:T(512)(128)(4,1)S(1)} %get-tuple-element.10), kind=kOutput, calls=%fused_computation.13 | convolution fusion | flops 302186496 | bytes 7864416 | tf_op jit(solution)/shard_map/vkc,krc->vkr/dot_general | solution.py:11
  578.2 85.5 %all-gather.17.cloned.1.call-done = f32[16,32768]{1,0:T(8,128)} async-done(((f32[16,1024]{1,0:T(8,128)}), f32[16,32768]{1,0:T(8,128)}) %all-gather.17.cloned.1.call-update) | async-done | bytes 2097168 | tf_op jit(solution)/shard_map/all_gather | solution.py:22
  663.7 1.7 copy_bitcast_fusion
  666.1 12.0 %convolution_bitcast_fusion = f32[16,96,128]{2,0,1:T(8,128)S(1)} fusion(f32[96,128,128]{2,1,0:T(8,128)} %bitcast.148, f32[96,16,128]{2,1,0:T(8,128)S(1)} %gather_fusion.5, pred[96]{0:T(512)(128)(4,1)S(1)} %get-tuple-element.10), kind=kOutput, calls=%fused_computation.12 | convolution fusion | flops 302186496 | bytes 7864416 | tf_op jit(solution)/shard_map/vkc,krc->vkr/dot_general | solution.py:11
  678.8 67.6 %psum.15 = f32[16]{0:T(128)S(1)} all-reduce(f32[16]{0:T(128)S(1)} %get-tuple-element.6), channel_id=1, replica_groups=mesh['blk'=4,'reader'=8,'bulk'=8] {'blk','reader'}, use_global_device_ids=true, to_apply=%region_3.5 | all-reduce | flops 16 | bytes 128 | tf_op jit(solution)/shard_map/psum | solution.py:49
  746.4 0.7 broadcast_divide_fusion
  (47 shorter events, 12.2 us)
Async XLA Ops:
  6.5 88.8 %all-gather.7.cloned.1.call-start = ((), (), s32[]{:S(2)}) async-start(), calls=%async_computation | async-start | bytes 2162688 | tf_op jit(solution)/shard_map/all_gather | solution.py:22
  7.3 189.2 %all-gather.9.cloned.1.call-start = ((), (), s32[]{:S(2)}) async-start(), calls=%async_computation.1 | async-start | bytes 2162688 | tf_op jit(solution)/shard_map/all_gather | solution.py:22
  97.8 12.6 %copy-start.2 = (f32[16,1024]{1,0:T(8,128)S(1)}, f32[16,1024]{1,0:T(8,128)}, u32[]{:S(2)}) copy-start(f32[16,1024]{1,0:T(8,128)} %param.8) | copy-start | bytes 196612
  111.0 186.7 %all-gather.11.cloned.1.call-start = ((), (), s32[]{:S(2)}) async-start(), calls=%async_computation.2 | async-start | bytes 2162688 | tf_op jit(solution)/shard_map/all_gather | solution.py:22
  199.0 12.6 %copy-start.1 = (f32[16,1024]{1,0:T(8,128)S(1)}, f32[16,1024]{1,0:T(8,128)}, u32[]{:S(2)}) copy-start(f32[16,1024]{1,0:T(8,128)} %fusion.49) | copy-start | bytes 196612
  212.2 249.0 %all-gather.13.cloned.1.call-start = ((), (), s32[]{:S(2)}) async-start(), calls=%async_computation.3 | async-start | bytes 2162688 | tf_op jit(solution)/shard_map/all_gather | solution.py:22
  300.1 12.6 %copy-start.4 = (f32[16,1024]{1,0:T(8,128)S(1)}, f32[16,1024]{1,0:T(8,128)}, u32[]{:S(2)}) copy-start(f32[16,1024]{1,0:T(8,128)} %fusion.48) | copy-start | bytes 196612
  381.1 181.3 %all-gather.15.cloned.1.call-start = ((), (), s32[]{:S(2)}) async-start(), calls=%async_computation.4 | async-start | bytes 2162688 | tf_op jit(solution)/shard_map/all_gather | solution.py:22
  476.9 186.7 %all-gather.17.cloned.1.call-start = ((), (), s32[]{:S(2)}) async-start(), calls=%async_computation.5 | async-start | bytes 2162688 | tf_op jit(solution)/shard_map/all_gather | solution.py:22
  564.9 12.6 %copy-start = (f32[16,1024]{1,0:T(8,128)S(1)}, f32[16,1024]{1,0:T(8,128)}, u32[]{:S(2)}) copy-start(f32[16,1024]{1,0:T(8,128)} %fusion.42) | copy-start | bytes 196612
  666.1 12.6 %copy-start.3 = (f32[16,1024]{1,0:T(8,128)S(1)}, f32[16,1024]{1,0:T(8,128)}, u32[]{:S(2)}) copy-start(f32[16,1024]{1,0:T(8,128)} %fusion.41) | copy-start | bytes 196612
Sparse Core Ops, SparseCore 0:
  9.1 86.1 all-gather.6
  111.1 85.3 all-gather.8
  212.3 85.3 all-gather.10
  381.3 79.9 all-gather.12
  477.1 85.3 all-gather.14
  578.3 85.3 all-gather.16
where the time goes:
time: 754 us
  waiting for transfers between devices  507 us (67%)
  blocking collectives  135 us (18%)
  matrix products  75.1 us (10%)
  local copies, waits for them, and re-layouts  16.4 us (2%)
  between operations  15 us (2%)
    all_gather x6, waiting for transfers between devices, apply_ham(): whole = lax.all_gather(current, ('blk', 'reader'), axis=1, tiled=True)  506 us
    psum x2, blocking collectives, shards(): squares = lax.psum(jnp.sum(third * third, axis=1), ('blk', 'reader'))  135 us
    dot_general x6, matrix products, contribute(): jnp.einsum('vkc,krc->vkr', sources, tiles, precision=lax.Precision.HIGHEST)  71.7 us
  transfers between devices with their start and end apart: 6, of which 6 were waited for; matrix products, arithmetic and copies ran while one was open for 0% of the time, Pallas kernels for 0%

commit v1 on v0

--- a/solution.py
+++ b/solution.py
@@ -5,6 +5,11 @@
 
 TILE = 128
 PASSES = 2
+
+
+def swapped_in(value, axis, dim):
+    sent = jnp.stack([value] * lax.axis_size(axis))
+    return jnp.concatenate(lax.all_to_all(sent, axis, 0, 0), axis=dim)
 
 
 def contribute(sources, tiles, rows, count):
@@ -19,7 +24,7 @@
     groups = tiles_here.shape[0]
     slots = tiles_here.shape[1]
     group_tiles = lax.axis_size("reader") * row_tiles
-    whole = lax.all_gather(current, ("blk", "reader"), axis=1, tiled=True)
+    whole = swapped_in(current, ("blk", "reader"), 1)
     tiled = whole.reshape(local_vecs, whole.shape[1] // TILE, TILE)
     offsets = (jnp.arange(groups, dtype=jnp.int32) * group_tiles)[:, None]
     glob = (offsets + cols_here).reshape(-1)

time: 754 us -> 453 us (0.60)
  waiting for transfers between devices: 507 us -> 26.7 us
  blocking collectives: 135 us -> 290 us
  local copies, waits for them, and re-layouts: 16.4 us -> 44.3 us
  between operations: 15 us -> 2.04 us
    all_gather x6 -> x0, waiting for transfers between devices: 506 us -> none  [apply_ham(): whole = lax.all_gather(current, ('blk', 'reader'), axis=1, tiled=True)]
    all_to_all x0 -> x5, blocking collectives: none -> 161 us  [swapped_in(): return jnp.concatenate(lax.all_to_all(sent, axis, 0, 0), axis=dim)]
    another operation x0 -> x18, local copies, waits for them, and re-layouts: none -> 29.6 us  [the longest x12 26 us: apply_ham(): tiled = whole.reshape(local_vecs, whole.shape[1] // TILE, TILE)]
    all_to_all x0 -> x1, waiting for transfers between devices: none -> 26.7 us  [swapped_in(): return jnp.concatenate(lax.all_to_all(sent, axis, 0, 0), axis=dim)]
  transfers between devices with their start and end apart: 6 -> 1, of which waited for: 6 -> 1; matrix products, arithmetic and copies ran while one was open for 0% -> 0% of each run, Pallas kernels for 0% -> 0%
where the time goes in v1:
time: 453 us; the launch traced here: 446 us
  blocking collectives  290 us (64%)
  matrix products  75 us (17%)
  local copies, waits for them, and re-layouts  44.3 us (10%)
  waiting for transfers between devices  26.7 us (6%)
  starting transfers between devices  7.45 us (2%)
    all_to_all x5, blocking collectives, swapped_in(): return jnp.concatenate(lax.all_to_all(sent, axis, 0, 0), axis=dim)  161 us
    psum x2, blocking collectives, shards(): squares = lax.psum(jnp.sum(third * third, axis=1), ('blk', 'reader'))  129 us
    dot_general x6, matrix products, contribute(): jnp.einsum('vkc,krc->vkr', sources, tiles, precision=lax.Precision.HIGHEST)  71.6 us
    all_to_all x1, waiting for transfers between devices, swapped_in(): return jnp.concatenate(lax.all_to_all(sent, axis, 0, 0), axis=dim)  26.7 us
    another operation x12, local copies, waits for them, and re-layouts, apply_ham(): tiled = whole.reshape(local_vecs, whole.shape[1] // TILE, TILE)  26 us
  transfers between devices with their start and end apart: 1, of which 1 were waited for; matrix products, arithmetic and copies ran while one was open for 0% of the time, Pallas kernels for 0%

profile of v1, /device:TPU:32, one launch (start us, length us, event | category | flops | bytes accessed | tf_op | source)
XLA Modules:
  0.0 446.4 jit_solution(16376240708065938581)
XLA Ops:
  0.0 2.4 stack.12
  2.4 7.5 %all-to-all-start = ((f32[32,16,1024]{2,1,0:T(8,128)}), f32[32,16,1024]{2,1,0:T(8,128)S(1)}, u32[]{:S(2)}, u32[]{:S(2)}) async-start(f32[32,16,1024]{2,1,0:T(8,128)} %stack.12), calls=%async_computation | async-start | bytes 4194304 | tf_op jit(solution)/shard_map/all_to_all | solution.py:12
  11.6 26.7 %all-to-all-done = f32[32,16,1024]{2,1,0:T(8,128)S(1)} async-done(((f32[32,16,1024]{2,1,0:T(8,128)}), f32[32,16,1024]{2,1,0:T(8,128)S(1)}, u32[]{:S(2)}, u32[]{:S(2)}) %all-to-all-start) | async-done | bytes 2097184 | tf_op jit(solution)/shard_map/all_to_all | solution.py:12
  38.3 2.6 copy.13
  42.6 2.6 copy.14
  45.1 2.2 gather_fusion
  47.4 12.0 %convolution_bitcast_fusion.5 = f32[16,96,128]{2,0,1:T(8,128)S(1)} fusion(f32[96,128,128]{2,1,0:T(8,128)} %bitcast.119, f32[96,16,128]{2,1,0:T(8,128)S(1)} %gather_fusion, pred[96]{0:T(512)(128)(4,1)S(1)} %get-tuple-element.10), kind=kOutput, calls=%fused_computation.11 | convolution fusion | flops 302186496 | bytes 7864416 | tf_op jit(solution)/shard_map/vkc,krc->vkr/dot_general | solution.py:16
  60.2 32.6 %all_to_all.30 = f32[32,16,1024]{2,1,0:T(8,128)S(1)} all-to-all(f32[32,16,1024]{2,1,0:T(8,128)S(1)} %stack.13), channel_id=1, replica_groups=mesh['blk'=4,'reader'=8,'bulk'=8] {'blk','reader'}, dimensions={0} | all-to-all | bytes 4194304 | tf_op jit(solution)/shard_map/all_to_all | solution.py:12
  95.5 2.8 copy.17
  99.0 11.9 %convolution_bitcast_fusion.4 = f32[16,96,128]{2,0,1:T(8,128)S(1)} fusion(f32[96,128,128]{2,1,0:T(8,128)} %bitcast.120, f32[96,16,128]{2,1,0:T(8,128)S(1)} %gather_fusion.1, pred[96]{0:T(512)(128)(4,1)S(1)} %get-tuple-element.10), kind=kOutput, calls=%fused_computation.10 | convolution fusion | flops 302186496 | bytes 7864416 | tf_op jit(solution)/shard_map/vkc,krc->vkr/dot_general | solution.py:16
  111.8 32.2 %all_to_all.31 = f32[32,16,1024]{2,1,0:T(8,128)S(1)} all-to-all(f32[32,16,1024]{2,1,0:T(8,128)S(1)} %stack.14), channel_id=1, replica_groups=mesh['blk'=4,'reader'=8,'bulk'=8] {'blk','reader'}, dimensions={0} | all-to-all | bytes 4194304 | tf_op jit(solution)/shard_map/all_to_all | solution.py:12
  146.7 2.8 copy.20
  150.2 11.9 %convolution_bitcast_fusion.3 = f32[16,96,128]{2,0,1:T(8,128)S(1)} fusion(f32[96,128,128]{2,1,0:T(8,128)} %bitcast.121, f32[96,16,128]{2,1,0:T(8,128)S(1)} %gather_fusion.2, pred[96]{0:T(512)(128)(4,1)S(1)} %get-tuple-element.10), kind=kOutput, calls=%fused_computation.9 | convolution fusion | flops 302186496 | bytes 7864416 | tf_op jit(solution)/shard_map/vkc,krc->vkr/dot_general | solution.py:16
  162.9 64.4 %psum.14 = f32[16]{0:T(128)S(1)} all-reduce(f32[16]{0:T(128)S(1)} %get-tuple-element.8), channel_id=1, replica_groups=mesh['blk'=4,'reader'=8,'bulk'=8] {'blk','reader'}, use_global_device_ids=true, to_apply=%region_1.3 | all-reduce | flops 16 | bytes 128 | tf_op jit(solution)/shard_map/psum | solution.py:54
  227.6 31.6 %all_to_all.32 = f32[32,16,1024]{2,1,0:T(8,128)S(1)} all-to-all(f32[32,16,1024]{2,1,0:T(8,128)S(1)} %stack.15), channel_id=1, replica_groups=mesh['blk'=4,'reader'=8,'bulk'=8] {'blk','reader'}, dimensions={0} | all-to-all | bytes 4194304 | tf_op jit(solution)/shard_map/all_to_all | solution.py:12
  261.9 2.8 copy.23
  265.5 11.9 %convolution_bitcast_fusion.2 = f32[16,96,128]{2,0,1:T(8,128)S(1)} fusion(f32[96,128,128]{2,1,0:T(8,128)} %bitcast.122, f32[96,16,128]{2,1,0:T(8,128)S(1)} %gather_fusion.3, pred[96]{0:T(512)(128)(4,1)S(1)} %get-tuple-element.10), kind=kOutput, calls=%fused_computation.8 | convolution fusion | flops 302186496 | bytes 7864416 | tf_op jit(solution)/shard_map/vkc,krc->vkr/dot_general | solution.py:16
  278.3 32.2 %all_to_all.33 = f32[32,16,1024]{2,1,0:T(8,128)S(1)} all-to-all(f32[32,16,1024]{2,1,0:T(8,128)S(1)} %stack.16), channel_id=1, replica_groups=mesh['blk'=4,'reader'=8,'bulk'=8] {'blk','reader'}, dimensions={0} | all-to-all | bytes 4194304 | tf_op jit(solution)/shard_map/all_to_all | solution.py:12
  313.3 2.8 copy.26
  316.8 11.9 %convolution_bitcast_fusion.1 = f32[16,96,128]{2,0,1:T(8,128)S(1)} fusion(f32[96,128,128]{2,1,0:T(8,128)} %bitcast.123, f32[96,16,128]{2,1,0:T(8,128)S(1)} %gather_fusion.4, pred[96]{0:T(512)(128)(4,1)S(1)} %get-tuple-element.10), kind=kOutput, calls=%fused_computation.7 | convolution fusion | flops 302186496 | bytes 7864416 | tf_op jit(solution)/shard_map/vkc,krc->vkr/dot_general | solution.py:16
  329.6 32.3 %all_to_all.34 = f32[32,16,1024]{2,1,0:T(8,128)S(1)} all-to-all(f32[32,16,1024]{2,1,0:T(8,128)S(1)} %stack.17), channel_id=1, replica_groups=mesh['blk'=4,'reader'=8,'bulk'=8] {'blk','reader'}, dimensions={0} | all-to-all | bytes 4194304 | tf_op jit(solution)/shard_map/all_to_all | solution.py:12
  364.7 2.8 copy.29
  368.2 11.9 %convolution_bitcast_fusion = f32[16,96,128]{2,0,1:T(8,128)S(1)} fusion(f32[96,128,128]{2,1,0:T(8,128)} %bitcast.124, f32[96,16,128]{2,1,0:T(8,128)S(1)} %gather_fusion.5, pred[96]{0:T(512)(128)(4,1)S(1)} %get-tuple-element.10), kind=kOutput, calls=%fused_computation.6 | convolution fusion | flops 302186496 | bytes 7864416 | tf_op jit(solution)/shard_map/vkc,krc->vkr/dot_general | solution.py:16
  380.8 64.4 %psum.15 = f32[16]{0:T(128)S(1)} all-reduce(f32[16]{0:T(128)S(1)} %get-tuple-element.6), channel_id=1, replica_groups=mesh['blk'=4,'reader'=8,'bulk'=8] {'blk','reader'}, use_global_device_ids=true, to_apply=%region_3.5 | all-reduce | flops 16 | bytes 128 | tf_op jit(solution)/shard_map/psum | solution.py:54
  (50 shorter events, 25.2 us)
Async XLA Ops:
  2.4 8.8 %copy-start.1 = (s32[1,4,24]{2,1,0:T(4,128)S(1)}, s32[1,4,24]{2,1,0:T(4,128)}, u32[]{:S(2)}) copy-start(s32[1,4,24]{2,1,0:T(4,128)} %param.10) | copy-start | bytes 1156
  2.4 8.9 %copy-start.2 = (s32[1,4,24]{2,1,0:T(4,128)S(1)}, s32[1,4,24]{2,1,0:T(4,128)}, u32[]{:S(2)}) copy-start(s32[1,4,24]{2,1,0:T(4,128)} %param.11) | copy-start | bytes 1156
  2.4 35.8 %all-to-all-start = ((f32[32,16,1024]{2,1,0:T(8,128)}), f32[32,16,1024]{2,1,0:T(8,128)S(1)}, u32[]{:S(2)}, u32[]{:S(2)}) async-start(f32[32,16,1024]{2,1,0:T(8,128)} %stack.12), calls=%async_computation | async-start | bytes 4194304 | tf_op jit(solution)/shard_map/all_to_all | solution.py:12
  47.4 12.6 %copy-start = (f32[16,1024]{1,0:T(8,128)S(1)}, f32[16,1024]{1,0:T(8,128)}, u32[]{:S(2)}) copy-start(f32[16,1024]{1,0:T(8,128)} %param.8) | copy-start | bytes 196612
